TPU v7x, 32 devices: a whole 2x2x4 slice. The times are simulated.
32 devices in a mesh: section: 4 (over y, x), tp: 4 (over z), mirror: 2 (over core).
Axes of the slice: x: 2, y: 2, z: 4, core: 2. Of those that a mesh axis runs over, the one named last changes fastest.
Arguments:
- feats: bfloat16 [2, 2, 128, 5120], P('mirror', None, 'tp'), may hold values from -16 to 16
- types: int32 [2, 2, 128], P('mirror', None, 'tp'), may hold values from 0 to 63
- segs: int32 [2, 2, 5, 128], P('mirror'), may hold values from 0 to 3, never falling along the last dimension, each value on 1 to 64 neighbouring positions
- type_table: bfloat16 [64, 5120], replicated, may hold values from -3 to 3
- gains: float32 [2, 4, 5120], P('mirror', 'section'), may hold values from 0.25 to 1.75, as said below
- w_qkv: bfloat16 [2, 4, 3, 5120, 512], P('mirror', 'section', None, None, 'tp'), may hold values from -8 to 8, as said below
- w_out: bfloat16 [2, 4, 512, 5120], P('mirror', 'section', 'tp'), as said below
- carry_acts: bfloat16 [2, 4, 128, 5120], P('mirror', 'section', 'tp'), may hold values from -16 to 16
- grad_in: bfloat16 [2, 4, 128, 5120], P('mirror', 'section', 'tp'), may hold values from -6 to 6
- saved: bfloat16 [2, 4, 2, 128, 5120], P('mirror', 'section', None, 'tp'), may hold values from -16 to 16
- cotangent: bfloat16 [2, 2, 128, 5120], P('mirror', None, 'tp'), may hold values from -6 to 6
Outputs:
- acts: bfloat16 [2, 4, 2, 128, 5120], P('mirror', 'section', None, 'tp')
- grad_acts: bfloat16 [2, 4, 2, 128, 5120], P('mirror', 'section', None, 'tp')
- grad_qkv: bfloat16 [2, 4, 3, 5120, 512], P('mirror', 'section', None, None, 'tp')
- grad_out: bfloat16 [2, 4, 512, 5120], P('mirror', 'section', 'tp')
Inputs may be any that keep to these rules, and one draw needn't show every extreme that they name: w_qkv[1, k] equals w_qkv[0, 3 - k]. w_out[1, k] equals w_out[0, 3 - k]. gains[1, k] equals gains[0, 3 - k]. `segs`: segment numbers never fall along a micro-batch; each segment holds at most half of 128 tokens, and one holds exactly that many.
All inputs are finite; a program needn't handle non-finite values.
Results may differ from a plain program's by a relative error of at most 0.015.
Values may be sent and summed in bfloat16 or wider, within the bound.
No kernel may reach another device: no remote copies, remote signals or barrier semaphores. Data moves between devices by JAX's collectives and lax.ppermute only.
A program may use at most 128 MiB of HBM per device.

v0:
```python
import math
import jax
import jax.numpy as jnp
from jax import lax
from jax.sharding import PartitionSpec as P

HD = 128


def passed_along(block, axis, distance):
    devices = range(lax.axis_size(axis))
    route = [(i - distance, i) for i in devices if i - distance in devices]
    return lax.ppermute(block, axis, route)


def swapped(value, axis, apart):
    return lax.ppermute(value, axis, [(i, i ^ 1 << apart) for i in range(lax.axis_size(axis))])


def normalize(values, gain_row):
    mean_square = jnp.mean(values * values, axis=-1, keepdims=True)
    return values * lax.rsqrt(mean_square + 1e-05) * gain_row


def segment_mask(segment_ids):
    position = jnp.arange(segment_ids.shape[0], dtype=jnp.int32)
    causal = position[None, :] <= position[:, None]
    return causal & (segment_ids[:, None] == segment_ids[None, :])


def attend(queries, keys_all, values_all, seg_mask):
    scores = jnp.einsum(
        "ihd,jhd->hij", queries, keys_all, preferred_element_type=jnp.float32
    ) / math.sqrt(queries.shape[-1])
    scores = jnp.where(seg_mask[None], scores, -1e30)
    highest = lax.stop_gradient(jnp.max(scores, axis=-1, keepdims=True))
    expo = jnp.exp(scores - highest)
    probs = (expo / jnp.sum(expo, axis=-1, keepdims=True)).astype(values_all.dtype)
    return jnp.einsum("hij,jhd->ihd", probs, values_all, preferred_element_type=jnp.float32)


def embedding(feat_rows, type_rows, type_table):
    onehot = (
        type_rows[:, None] == jnp.arange(type_table.shape[0], dtype=jnp.int32)[None, :]
    ).astype(jnp.bfloat16)
    looked = jnp.dot(onehot, type_table, preferred_element_type=jnp.float32)
    return (feat_rows.astype(jnp.float32) + looked).astype(jnp.bfloat16)


def shards(
    feats, types, segs, type_table, gains, w_qkv, w_out, carry_acts, grad_in, saved, cotangent
):
    sections = lax.axis_size("section")
    section_index = lax.axis_index("section")
    on_first_pipe = lax.axis_index("mirror") == 0
    position = jnp.where(on_first_pipe, section_index, sections - 1 - section_index)
    gain_row = gains[0, 0]
    qkv_weight = w_qkv[0, 0]
    out_weight = w_out[0, 0]
    window_steps = feats.shape[1]
    seq_len = segs.shape[3]
    model_width = qkv_weight.shape[1]
    inner_here = qkv_weight.shape[-1]
    heads_here = inner_here // HD

    def mask_for(which, index):
        return segment_mask(lax.dynamic_index_in_dim(segs[0, which], index, 0, keepdims=False))

    def backward_layer(layer_in, upstream, seg_mask):
        normed = normalize(layer_in.astype(jnp.float32), gain_row).astype(jnp.bfloat16)
        normed_full, upstream_full = (
            lax.all_gather(normed, "tp", axis=0, tiled=True),
            lax.all_gather(upstream, "tp", axis=0, tiled=True),
        )
        projected = jnp.einsum(
            "sd,cdn->csn", normed_full, qkv_weight, preferred_element_type=jnp.float32
        ).astype(jnp.bfloat16)
        heads_view = projected.reshape(3, seq_len, heads_here, HD)
        primal, pull_attend = jax.vjp(
            lambda query_part, key_part, value_part: attend(
                query_part, key_part, value_part, seg_mask
            ),
            heads_view[0],
            heads_view[1],
            heads_view[2],
        )
        mixed = primal.reshape(seq_len, inner_here).astype(jnp.bfloat16)
        d_mixed = jnp.einsum(
            "sd,nd->sn", upstream_full, out_weight, preferred_element_type=jnp.float32
        ).astype(jnp.bfloat16)
        pulled = pull_attend(d_mixed.astype(jnp.float32).reshape(seq_len, heads_here, HD))
        d_projected = jnp.stack(pulled).reshape(3, seq_len, inner_here)
        d_normed = lax.psum_scatter(
            jnp.einsum(
                "csn,cdn->sd", d_projected, qkv_weight, preferred_element_type=jnp.float32
            ).astype(jnp.bfloat16),
            "tp",
            scatter_dimension=0,
            tiled=True,
        )
        unused_norm, pull_norm = jax.vjp(
            lambda inputs: normalize(inputs, gain_row), layer_in.astype(jnp.float32)
        )
        d_input = pull_norm(d_normed.astype(jnp.float32))[0]
        result = (upstream.astype(jnp.float32) + d_input).astype(jnp.bfloat16)
        qkv_term = jnp.einsum(
            "sd,csn->cdn", normed_full, d_projected, preferred_element_type=jnp.float32
        )
        out_term = jnp.einsum("sn,sd->nd", mixed, upstream_full, preferred_element_type=jnp.float32)
        return (result, qkv_term, out_term)

    forward_in = carry_acts[0, 0]
    backward_in = grad_in[0, 0]
    forward_outs = []
    backward_outs = []
    qkv_total = jnp.zeros(qkv_weight.shape, jnp.float32)
    out_total = jnp.zeros(out_weight.shape, jnp.float32)
    for step_index in range(window_steps):
        embedded = embedding(feats[0, step_index], types[0, step_index], type_table)
        current = jnp.where(position == 0, embedded, forward_in)
        forward_normed = normalize(current.astype(jnp.float32), gain_row).astype(jnp.bfloat16)
        forward_normed_full = lax.all_gather(forward_normed, "tp", axis=0, tiled=True)
        forward_projected = jnp.einsum(
            "sd,cdn->csn", forward_normed_full, qkv_weight, preferred_element_type=jnp.float32
        ).astype(jnp.bfloat16)
        forward_heads_view = forward_projected.reshape(3, seq_len, heads_here, HD)
        forward_mixed = (
            attend(
                forward_heads_view[0],
                forward_heads_view[1],
                forward_heads_view[2],
                mask_for(0, step_index - position + sections - 1),
            )
            .reshape(seq_len, inner_here)
            .astype(jnp.bfloat16)
        )
        attn_rows = lax.psum_scatter(
            jnp.dot(forward_mixed, out_weight, preferred_element_type=jnp.float32).astype(
                jnp.bfloat16
            ),
            "tp",
            scatter_dimension=0,
            tiled=True,
        ).astype(jnp.float32)
        forward_out = (current.astype(jnp.float32) + attn_rows).astype(jnp.bfloat16)
        upstream = jnp.where(position == sections - 1, cotangent[0, step_index], backward_in)
        backward_out, qkv_term, out_term = backward_layer(
            saved[0, 0, step_index], upstream, mask_for(1, step_index + position)
        )
        qkv_total = qkv_total + qkv_term
        out_total = out_total + out_term
        forward_outs.append(forward_out)
        backward_outs.append(backward_out)
        if step_index + 1 < window_steps:
            toward_higher = jnp.where(on_first_pipe, forward_out, backward_out)
            toward_lower = jnp.where(on_first_pipe, backward_out, forward_out)
            from_lower = passed_along(toward_higher, "section", 1)
            from_upper = passed_along(toward_lower, "section", -1)
            forward_in = jnp.where(on_first_pipe, from_lower, from_upper)
            backward_in = jnp.where(on_first_pipe, from_upper, from_lower)
    qkv_size = qkv_total.size
    own_terms = jnp.concatenate(
        [qkv_total.astype(jnp.bfloat16).reshape(-1), out_total.astype(jnp.bfloat16).reshape(-1)]
    )
    bit_count = lax.axis_size(("section", "mirror")).bit_length() - 1
    partner = own_terms
    for bit_number in range(bit_count):
        partner = swapped(partner, ("section", "mirror"), bit_number)
    summed = (own_terms.astype(jnp.float32) + partner.astype(jnp.float32)).astype(jnp.bfloat16)
    grad_qkv = summed[:qkv_size].reshape(3, model_width, inner_here)
    grad_out = summed[qkv_size:].reshape(inner_here, model_width)
    acts_block = jnp.stack(forward_outs)[None, None]
    grads_block = jnp.stack(backward_outs)[None, None]
    return (acts_block, grads_block, grad_qkv[None, None], grad_out[None, None])


def solution(mesh):
    in_specs = (
        P("mirror", None, "tp", None),
        P("mirror", None, "tp"),
        P("mirror", None, None, None),
        P(),
        P("mirror", "section", None),
        P("mirror", "section", None, None, "tp"),
        P("mirror", "section", "tp", None),
        P("mirror", "section", "tp", None),
        P("mirror", "section", "tp", None),
        P("mirror", "section", None, "tp", None),
        P("mirror", None, "tp", None),
    )
    out_specs = (
        P("mirror", "section", None, "tp", None),
        P("mirror", "section", None, "tp", None),
        P("mirror", "section", None, None, "tp"),
        P("mirror", "section", "tp", None),
    )
    return jax.shard_map(shards, mesh=mesh, in_specs=in_specs, out_specs=out_specs, check_vma=False)
```

profile of v0, /device:TPU:0, one launch (start us, length us, event | category | flops | bytes accessed | tf_op | source)
XLA Modules:
  0.0 553.4 jit_solution(733608073758702413)
XLA Ops:
  11.4 34.4 %all-gather.10.cloned.1.call-done = bf16[128,5120]{1,0:T(8,128)(2,1)} async-done(((bf16[32,5120]{1,0:T(8,128)(2,1)}), bf16[128,5120]{1,0:T(8,128)(2,1)}) %all-gather.10.cloned.1.call-update) | async-done | bytes 1310736 | tf_op jit(solution)/shard_map/all_gather | solution.py:72
  45.8 3.4 fusion.65
  49.4 30.3 %all-gather.18.cloned.1.call-done = bf16[1,1,128,5120]{3,2,1,0:T(8,128)(2,1)} async-done(((bf16[1,1,32,5120]{3,2,1,0:T(8,128)(2,1)}), bf16[1,1,128,5120]{3,2,1,0:T(8,128)(2,1)}) %all-gather.18.cloned.1.call-update) | async-done | bytes 1310736 | tf_op jit(solution)/shard_map/all_gather | solution.py:73
  82.3 4.5 fusion.2
  88.0 2.0 multiply_reduce_fusion
  90.1 27.4 %reduce-scatter.7.cloned.1.call-done = bf16[32,5120]{1,0:T(8,128)(2,1)} async-done(((bf16[128,5120]{1,0:T(8,128)(2,1)}), bf16[32,5120]{1,0:T(8,128)(2,1)}) %reduce-scatter.7.cloned.1.call-update) | async-done | bytes 327696 | tf_op jit(solution)/shard_map/reduce_scatter | solution.py:93
  121.6 30.7 %all-gather.8.cloned.1.call-done = bf16[128,5120]{1,0:T(8,128)(2,1)} async-done(((bf16[32,5120]{1,0:T(8,128)(2,1)}), bf16[128,5120]{1,0:T(8,128)(2,1)}) %all-gather.8.cloned.1.call-update) | async-done | bytes 1310736 | tf_op jit(solution)/shard_map/all_gather | solution.py:122
  152.3 3.4 fusion.70
  159.5 28.8 %reduce-scatter.5.cloned.1.call-done = bf16[32,5120]{1,0:T(8,128)(2,1)} async-done(((bf16[128,5120]{1,0:T(8,128)(2,1)}), bf16[32,5120]{1,0:T(8,128)(2,1)}) %reduce-scatter.5.cloned.1.call-update) | async-done | bytes 327696 | tf_op jit(solution)/shard_map/reduce_scatter | solution.py:137
  190.6 3.5 collective-permute-start
  195.4 5.2 collective-permute-done
  200.6 9.0 %collective-permute-done.1 = bf16[32,5120]{1,0:T(8,128)(2,1)S(1)} collective-permute-done((bf16[32,5120]{1,0:T(8,128)(2,1)S(1)}, bf16[32,5120]{1,0:T(8,128)(2,1)S(1)}, u32[]{:S(2)}, u32[]{:S(2)}) %collective-permute-start.1) | collective-permute-done | bytes 327712 | tf_op jit(solution)/shard_map/ppermute | solution.py:13
  211.4 2.1 fusion.25
  213.5 5.6 %fusion.22 = f32[3,128,5120]{2,1,0:T(8,128)} fusion(bf16[128,5120]{1,0:T(8,128)(2,1)} %all-gather.10.cloned.1.call-done, bf16[1,128,1,128]{3,1,2,0:T(8,128)(2,1)} %copy-done.19, bf16[1,128,1,128]{3,1,2,0:T(8,128)(2,1)S(1)} %fusion.91, bf16[1,128,1,128]{3,1,2,0:T(8,128)(2,1)S(1)} %fusion.90), kind=kOutput, calls=%fused_computation.32 | convolution fusion | flops 503414784 | bytes 9273344 | tf_op jit(solution)/shard_map/sd,csn->cdn/dot_general | solution.py:106
  219.2 2.4 all-gather.16.cloned.1.call-done
  221.6 3.4 fusion.55
  225.2 30.3 %all-gather.14.cloned.1.call-done = bf16[128,5120]{1,0:T(8,128)(2,1)} async-done(((bf16[32,5120]{1,0:T(8,128)(2,1)}), bf16[128,5120]{1,0:T(8,128)(2,1)}) %all-gather.14.cloned.1.call-update) | async-done | bytes 1310736 | tf_op jit(solution)/shard_map/all_gather | solution.py:73
  258.7 3.5 fusion.18
  263.9 6.4 %fusion = bf16[3,5120,128]{1,2,0:T(8,128)(2,1)} fusion(f32[3,128,5120]{2,1,0:T(8,128)} %fusion.22, bf16[128,5120]{1,0:T(8,128)(2,1)S(1)} %copy-done.4, bf16[1,128,1,128]{3,1,2,0:T(8,128)(2,1)S(1)} %copy-done.20, bf16[1,128,1,128]{3,1,2,0:T(8,128)(2,1)S(1)} %fusion.94, bf16[1,128,1,128]{3,1,2,0:T(8,128)(2,1)S(1)} %fusion.93), kind=kOutput, calls=%fused_computation.2 | convolution fusion | flops 507346944 | bytes 13205504 | tf_op jit(solution)/shard_map/sd,csn->cdn/dot_general | solution.py:106
  270.3 6.3 %copy.23 = bf16[3,5120,128]{2,1,0:T(8,128)(2,1)} copy(bf16[3,5120,128]{1,2,0:T(8,128)(2,1)} %fusion) | data formatting | bytes 7864320 | tf_op jit(solution)/shard_map/convert_element_type | solution.py:163
  276.6 14.2 %pad_maximum_fusion = bf16[2621440]{0:T(1024)(128)(2,1)} fusion(bf16[655360]{0:T(1024)(128)(2,1)S(1)} %bitcast.314, bf16[1966080]{0:T(1024)(128)(2,1)} %bitcast.312), kind=kLoop, calls=%fused_computation.17 | loop fusion | flops 10485760 | bytes 10485760 | tf_op jit(solution)/shard_map/concatenate | solution.py:162
  290.7 2.4 fusion.3
  293.2 6.5 %collective-permute-done.2 = bf16[2621440]{0:T(1024)(128)(2,1)} collective-permute-done((bf16[2621440]{0:T(1024)(128)(2,1)}, bf16[2621440]{0:T(1024)(128)(2,1)}, u32[]{:S(2)}, u32[]{:S(2)}) %collective-permute-start.2) | collective-permute-done | bytes 5242912 | tf_op jit(solution)/shard_map/ppermute | solution.py:17
  301.2 2.4 fusion.109
  303.6 20.3 %reduce-scatter.11.cloned.1.call-done = bf16[32,5120]{1,0:T(8,128)(2,1)} async-done(((bf16[128,5120]{1,0:T(8,128)(2,1)}), bf16[32,5120]{1,0:T(8,128)(2,1)}) %reduce-scatter.11.cloned.1.call-update) | async-done | bytes 327696 | tf_op jit(solution)/shard_map/reduce_scatter | solution.py:93
  325.1 2.3 fusion.123
  327.8 87.3 %collective-permute-done.3 = bf16[2621440]{0:T(1024)(128)(2,1)} collective-permute-done((bf16[2621440]{0:T(1024)(128)(2,1)}, bf16[2621440]{0:T(1024)(128)(2,1)}, u32[]{:S(2)}, u32[]{:S(2)}) %collective-permute-start.3) | collective-permute-done | bytes 5242912 | tf_op jit(solution)/shard_map/ppermute | solution.py:17
  416.6 3.4 fusion.60
  424.8 26.9 %reduce-scatter.9.cloned.1.call-done = bf16[32,5120]{1,0:T(8,128)(2,1)} async-done(((bf16[128,5120]{1,0:T(8,128)(2,1)}), bf16[32,5120]{1,0:T(8,128)(2,1)}) %reduce-scatter.9.cloned.1.call-update) | async-done | bytes 327696 | tf_op jit(solution)/shard_map/reduce_scatter | solution.py:137
  453.8 75.9 %collective-permute-done.4 = bf16[2621440]{0:T(1024)(128)(2,1)} collective-permute-done((bf16[2621440]{0:T(1024)(128)(2,1)}, bf16[2621440]{0:T(1024)(128)(2,1)}, u32[]{:S(2)}, u32[]{:S(2)}) %collective-permute-start.4) | collective-permute-done | bytes 5242912 | tf_op jit(solution)/shard_map/ppermute | solution.py:17
  529.7 13.3 %add_convert_fusion = bf16[2621440]{0:T(1024)(128)(2,1)S(1)} fusion(bf16[2621440]{0:T(1024)(128)(2,1)} %collective-permute-done.4, bf16[655360]{0:T(1024)(128)(2,1)S(1)} %bitcast.315, bf16[1966080]{0:T(1024)(128)(2,1)} %bitcast.313), kind=kLoop, calls=%fused_computation | loop fusion | flops 18350080 | bytes 15728640 | tf_op jit(solution)/shard_map/convert_element_type | solution.py:169
  543.1 2.1 slice.133
  (129 shorter events, 39.4 us)
Async XLA Ops:
  7.2 72.5 %copy-start = (bf16[1,1,128,5120]{3,2,1,0:T(8,128)(2,1)S(1)}, bf16[1,1,128,5120]{3,2,1,0:T(8,128)(2,1)}, u32[]{:S(2)}) copy-start(bf16[1,1,128,5120]{3,2,1,0:T(8,128)(2,1)} %param.17) | copy-start | bytes 3932164
  7.2 3.3 copy-start.13
  7.2 3.3 copy-start.16
  7.2 4.2 copy-start.21
  7.2 38.6 %all-gather.10.cloned.1.call-start = ((), (), s32[]{:S(2)}) async-start(), calls=%async_computation.6 | async-start | bytes 1638400 | tf_op jit(solution)/shard_map/all_gather | solution.py:72
  8.5 2.8 copy-start.23
  10.5 69.3 %all-gather.18.cloned.1.call-start = ((), (), s32[]{:S(2)}) async-start(), calls=%async_computation.13 | async-start | bytes 1638400 | tf_op jit(solution)/shard_map/all_gather | solution.py:73
  11.3 106.1 %reduce-scatter.7.cloned.1.call-start = ((), (), s32[]{:S(2)}) async-start(), calls=%async_computation.7 | async-start | bytes 1638400 | tf_op jit(solution)/shard_map/reduce_scatter | solution.py:93
  86.9 30.6 %copy-start.2 = (bf16[1,1,2,32,5120]{4,3,2,1,0:T(8,128)(2,1)S(1)}, bf16[1,1,2,32,5120]{4,3,2,1,0:T(8,128)(2,1)}, u32[]{:S(2)}) copy-start(bf16[1,1,2,32,5120]{4,3,2,1,0:T(8,128)(2,1)} %param.20) | copy-start | bytes 1966084
  86.9 30.6 %copy-start.12 = (f32[1,1,5120]{2,1,0:T(1,128)S(1)}, f32[1,1,5120]{2,1,0:T(1,128)}, u32[]{:S(2)}) copy-start(f32[1,1,5120]{2,1,0:T(1,128)} %param.15) | copy-start | bytes 61444
  86.9 65.4 %all-gather.8.cloned.1.call-start = ((), (), s32[]{:S(2)}) async-start(), calls=%async_computation.4 | async-start | bytes 1638400 | tf_op jit(solution)/shard_map/all_gather | solution.py:122
  121.0 67.4 %reduce-scatter.5.cloned.1.call-start = ((), (), s32[]{:S(2)}) async-start(), calls=%async_computation.5 | async-start | bytes 1638400 | tf_op jit(solution)/shard_map/reduce_scatter | solution.py:137
  157.7 30.6 %copy-start.10 = (bf16[1,1,32,5120]{3,2,1,0:T(8,128)(2,1)S(1)}, bf16[1,1,32,5120]{3,2,1,0:T(8,128)(2,1)}, u32[]{:S(2)}) copy-start(bf16[1,1,32,5120]{3,2,1,0:T(8,128)(2,1)} %slice_select_fusion) | copy-start | bytes 983044
  157.7 30.6 %copy-start.11 = (bf16[32,5120]{1,0:T(8,128)(2,1)S(1)}, bf16[32,5120]{1,0:T(8,128)(2,1)}, u32[]{:S(2)}) copy-start(bf16[32,5120]{1,0:T(8,128)(2,1)} %reduce-scatter.7.cloned.1.call-done) | copy-start | bytes 983044
  157.7 63.9 %all-gather.16.cloned.1.call-start = ((), (), s32[]{:S(2)}) async-start(), calls=%async_computation.11 | async-start | bytes 1638400 | tf_op jit(solution)/shard_map/all_gather | solution.py:72
  159.5 95.9 %all-gather.14.cloned.1.call-start = ((), (), s32[]{:S(2)}) async-start(), calls=%async_computation.10 | async-start | bytes 1638400 | tf_op jit(solution)/shard_map/all_gather | solution.py:73
  188.3 22.0 %copy-start.14 = (bf16[1,2,32,5120]{3,2,1,0:T(8,128)(2,1)S(1)}, bf16[1,2,32,5120]{3,2,1,0:T(8,128)(2,1)}, u32[]{:S(2)}) copy-start(bf16[1,2,32,5120]{3,2,1,0:T(8,128)(2,1)} %param.21) | copy-start | bytes 1966084
  190.4 20.9 %copy-start.3 = (bf16[1,1,128,5120]{3,2,1,0:T(8,128)(2,1)S(1)}, bf16[1,1,128,5120]{3,2,1,0:T(8,128)(2,1)}, u32[]{:S(2)}) copy-start(bf16[1,1,128,5120]{3,2,1,0:T(8,128)(2,1)} %all-gather.18.cloned.1.call-done) | copy-start | bytes 3932164
  190.6 10.1 %collective-permute-start = (bf16[32,5120]{1,0:T(8,128)(2,1)S(1)}, bf16[32,5120]{1,0:T(8,128)(2,1)S(1)}, u32[]{:S(2)}, u32[]{:S(2)}) collective-permute-start(bf16[32,5120]{1,0:T(8,128)(2,1)S(1)} %broadcast_select_fusion.1), channel_id=1, source_target_pairs={{0,8},{8,16},{16,24},{1,9},{9,17},{17,25},{2,10},{10,18},{18,26},{... | collective-permute-start | bytes 983048 | tf_op jit(solution)/shard_map/ppermute | solution.py:13
  194.1 15.5 %collective-permute-start.1 = (bf16[32,5120]{1,0:T(8,128)(2,1)S(1)}, bf16[32,5120]{1,0:T(8,128)(2,1)S(1)}, u32[]{:S(2)}, u32[]{:S(2)}) collective-permute-start(bf16[32,5120]{1,0:T(8,128)(2,1)S(1)} %get-tuple-element.6), channel_id=1, source_target_pairs={{8,0},{16,8},{24,16},{9,1},{17,9},{25,17},{10,2},{18,10},{26,18},{... | collective-permute-start | bytes 983048 | tf_op jit(solution)/shard_map/ppermute | solution.py:13
  200.6 9.0 %copy-start.17 = (bf16[32,5120]{1,0:T(8,128)(2,1)}, bf16[32,5120]{1,0:T(8,128)(2,1)S(1)}, u32[]{:S(2)}) copy-start(bf16[32,5120]{1,0:T(8,128)(2,1)S(1)} %collective-permute-done) | copy-start | bytes 983044
  211.1 112.8 %reduce-scatter.11.cloned.1.call-start = ((), (), s32[]{:S(2)}) async-start(), calls=%async_computation.12 | async-start | bytes 1638400 | tf_op jit(solution)/shard_map/reduce_scatter | solution.py:93
  255.4 3.3 copy-start.5
  276.6 14.2 %copy-start.1 = (bf16[1,1,3,5120,128]{4,3,2,1,0:T(8,128)(2,1)S(1)}, bf16[1,1,3,5120,128]{4,3,2,1,0:T(8,128)(2,1)}, u32[]{:S(2)}) copy-start(bf16[1,1,3,5120,128]{4,3,2,1,0:T(8,128)(2,1)} %param.16) | copy-start | bytes 11796484
  290.7 9.0 %collective-permute-start.2 = (bf16[2621440]{0:T(1024)(128)(2,1)}, bf16[2621440]{0:T(1024)(128)(2,1)}, u32[]{:S(2)}, u32[]{:S(2)}) collective-permute-start(bf16[2621440]{0:T(1024)(128)(2,1)} %pad_maximum_fusion), channel_id=1, source_target_pairs={{0,1},{1,0},{8,9},{9,8},{16,17},{17,16},{24,25},{25,24},{2,3},{3,2... | collective-permute-start | bytes 15728648 | tf_op jit(solution)/shard_map/ppermute | solution.py:17
  293.1 8.1 %copy-start.25 = (s32[32]{0:T(128)S(1)}, s32[32]{0:T(128)}, u32[]{:S(2)}) copy-start(s32[32]{0:T(128)} %get-tuple-element.19) | copy-start | bytes 388
  293.1 123.4 %all-gather.12.cloned.1.call-start = ((), (), s32[]{:S(2)}) async-start(), calls=%async_computation.8 | async-start | bytes 1638400 | tf_op jit(solution)/shard_map/all_gather | solution.py:122
  299.7 115.4 %collective-permute-start.3 = (bf16[2621440]{0:T(1024)(128)(2,1)}, bf16[2621440]{0:T(1024)(128)(2,1)}, u32[]{:S(2)}, u32[]{:S(2)}) collective-permute-start(bf16[2621440]{0:T(1024)(128)(2,1)} %collective-permute-done.2), channel_id=1, source_target_pairs={{0,8},{1,9},{8,0},{9,1},{16,24},{17,25},{24,16},{25,17},{2,10},{3,... | collective-permute-start | bytes 15728648 | tf_op jit(solution)/shard_map/ppermute | solution.py:17
  327.5 92.5 %copy-start.26 = (s32[128]{0:T(128)S(1)}, s32[128]{0:T(128)}, u32[]{:S(2)}) copy-start(s32[128]{0:T(128)} %get-tuple-element.17) | copy-start | bytes 1540
  327.5 124.2 %reduce-scatter.9.cloned.1.call-start = ((), (), s32[]{:S(2)}) async-start(), calls=%async_computation.9 | async-start | bytes 1638400 | tf_op jit(solution)/shard_map/reduce_scatter | solution.py:137
  415.1 114.5 %collective-permute-start.4 = (bf16[2621440]{0:T(1024)(128)(2,1)}, bf16[2621440]{0:T(1024)(128)(2,1)}, u32[]{:S(2)}, u32[]{:S(2)}) collective-permute-start(bf16[2621440]{0:T(1024)(128)(2,1)} %collective-permute-done.3), channel_id=1, source_target_pairs={{0,16},{1,17},{8,24},{9,25},{16,0},{17,1},{24,8},{25,9},{2,18},{3,... | collective-permute-start | bytes 15728648 | tf_op jit(solution)/shard_map/ppermute | solution.py:17
  422.0 30.9 %copy-start.7 = (bf16[32,5120]{1,0:T(8,128)(2,1)S(1)}, bf16[32,5120]{1,0:T(8,128)(2,1)}, u32[]{:S(2)}) copy-start(bf16[32,5120]{1,0:T(8,128)(2,1)} %copy-done.6) | copy-start | bytes 983044
  (10 other events, 9.8 us)
Sparse Core Ops, SparseCore 0:
  10.6 35.2 all-gather.9
  48.0 31.6 all-gather.17
  87.0 30.4 reduce-scatter.6
  121.1 31.1 all-gather.7
  157.8 30.4 reduce-scatter.4
  190.3 31.1 all-gather.15
  223.7 31.6 all-gather.13
  293.3 30.6 reduce-scatter.10
  327.6 31.1 all-gather.11
  422.1 29.5 reduce-scatter.8
where the time goes:
time: 554 us; the launch traced here: 553 us
  waiting for transfers between devices  416 us (75%)
  matrix products  52.3 us (9%)
  other arithmetic  46.1 us (8%)
  local copies, waits for them, and re-layouts  16.3 us (3%)
  between operations  14.5 us (3%)
  starting transfers between devices  8.56 us (2%)
    ppermute x3, waiting for transfers between devices, swapped(): lax.ppermute(value, axis, [(i, i ^ 1 << apart) for i in range(lax.axis_si...  170 us
    all_gather x2, waiting for transfers between devices, backward_layer(): lax.all_gather(upstream, 'tp', axis=0, tiled=True)  60.5 us
    reduce_scatter x2, waiting for transfers between devices, shards(): lax.psum_scatter(jnp.dot(forward_mixed, out_weight, preferred_element_typ...  55.7 us
    reduce_scatter x2, waiting for transfers between devices, backward_layer(): lax.psum_scatter(jnp.einsum('csn,cdn->sd', d_projected, qkv_weight, prefe...  47.7 us
    all_gather x2, waiting for transfers between devices, backward_layer(): lax.all_gather(normed, 'tp', axis=0, tiled=True)  36.8 us
    all_gather x2, waiting for transfers between devices, shards(): lax.all_gather(forward_normed, 'tp', axis=0, tiled=True)  30.7 us
    ppermute x2, waiting for transfers between devices, passed_along(): return lax.ppermute(block, axis, route)  14.2 us
    concatenate x1, other arithmetic, shards(): jnp.concatenate([qkv_total.astype(jnp.bfloat16).reshape(-1), out_total.as...  14.2 us
  transfers between devices with their start and end apart: 15, of which 14 were waited for; matrix products, arithmetic and copies ran while one was open for 7% of the time, Pallas kernels for 0%

commit v1 on v0

--- a/solution.py
+++ b/solution.py
@@ -5,6 +5,20 @@
 from jax.sharding import PartitionSpec as P
 
 HD = 128
+
+
+def on_each_block(x, axis, dim, make, out_dim):
+    ways, here, step = (lax.axis_size(axis), lax.axis_index(axis), x.shape[dim])
+    earlier, later = ([], [])
+    going_up = going_down = x
+    for far in range(ways // 2 + 1):
+        earlier.append(make(going_up, (here - far) % ways * step))
+        if 0 < far < ways - ways // 2:
+            later.append(make(going_down, (here + far) % ways * step))
+        going_up = lax.ppermute(going_up, axis, [(d, (d + 1) % ways) for d in range(ways)])
+        going_down = lax.ppermute(going_down, axis, [(d, (d - 1) % ways) for d in range(ways)])
+    line = jnp.concatenate([*earlier[::-1], *later], axis=out_dim)
+    return jnp.roll(line, (here - ways // 2) * earlier[0].shape[out_dim], axis=out_dim)
 
 
 def passed_along(block, axis, distance):
@@ -119,9 +133,14 @@
         embedded = embedding(feats[0, step_index], types[0, step_index], type_table)
         current = jnp.where(position == 0, embedded, forward_in)
         forward_normed = normalize(current.astype(jnp.float32), gain_row).astype(jnp.bfloat16)
-        forward_normed_full = lax.all_gather(forward_normed, "tp", axis=0, tiled=True)
-        forward_projected = jnp.einsum(
-            "sd,cdn->csn", forward_normed_full, qkv_weight, preferred_element_type=jnp.float32
+        forward_projected = on_each_block(
+            forward_normed,
+            "tp",
+            0,
+            lambda part, start: jnp.einsum(
+                "sd,cdn->csn", part, qkv_weight, preferred_element_type=jnp.float32
+            ),
+            1,
         ).astype(jnp.bfloat16)
         forward_heads_view = forward_projected.reshape(3, seq_len, heads_here, HD)
         forward_mixed = (

time: 554 us -> 548 us (0.989)
  waiting for transfers between devices: 416 us -> 400 us
    ppermute x0 -> x6, waiting for transfers between devices: none -> 32.8 us  [the longest x4 32.8 us: on_each_block(): lax.ppermute(going_up, axis, [(d, (d + 1) % ways) for d in range(ways)])]
    all_gather x2 -> x0, waiting for transfers between devices: 30.7 us -> none  [shards(): lax.all_gather(forward_normed, 'tp', axis=0, tiled=True)]
    ppermute x3, waiting for transfers between devices: 170 us -> 146 us  [swapped(): lax.ppermute(value, axis, [(i, i ^ 1 << apart) for i in range(lax.axis_si...]
    reduce_scatter x2, waiting for transfers between devices: 47.7 us -> 55.1 us  [backward_layer(): lax.psum_scatter(jnp.einsum('csn,cdn->sd', d_projected, qkv_weight, prefe...]
  transfers between devices with their start and end apart: 15 -> 19, of which waited for: 14 -> 16; matrix products, arithmetic and copies ran while one was open for 7% -> 9% of each run, Pallas kernels for 0% -> 0%
where the time goes in v1:
time: 548 us; the launch traced here: 547 us
  waiting for transfers between devices  400 us (73%)
  matrix products  56.6 us (10%)
  other arithmetic  45.7 us (8%)
  local copies, waits for them, and re-layouts  17.2 us (3%)
  between operations  14.6 us (3%)
  starting transfers between devices  13.3 us (2%)
    ppermute x3, waiting for transfers between devices, swapped(): lax.ppermute(value, axis, [(i, i ^ 1 << apart) for i in range(lax.axis_si...  146 us
    all_gather x2, waiting for transfers between devices, backward_layer(): lax.all_gather(upstream, 'tp', axis=0, tiled=True)  60.3 us
    reduce_scatter x2, waiting for transfers between devices, shards(): lax.psum_scatter(jnp.dot(forward_mixed, out_weight, preferred_element_typ...  56.7 us
    reduce_scatter x2, waiting for transfers between devices, backward_layer(): lax.psum_scatter(jnp.einsum('csn,cdn->sd', d_projected, qkv_weight, prefe...  55.1 us
    all_gather x2, waiting for transfers between devices, backward_layer(): lax.all_gather(normed, 'tp', axis=0, tiled=True)  34.5 us
    ppermute x4, waiting for transfers between devices, on_each_block(): lax.ppermute(going_up, axis, [(d, (d + 1) % ways) for d in range(ways)])  32.8 us
    ppermute x2, waiting for transfers between devices, passed_along(): return lax.ppermute(block, axis, route)  14.2 us
    convert_element_type x1, other arithmetic, shards(): (own_terms.astype(jnp.float32) + partner.astype(jnp.float32)).astype(jnp....  13.3 us
  transfers between devices with their start and end apart: 19, of which 16 were waited for; matrix products, arithmetic and copies ran while one was open for 9% of the time, Pallas kernels for 0%

profile of v1, /device:TPU:0, one launch (start us, length us, event | category | flops | bytes accessed | tf_op | source)
XLA Modules:
  0.0 547.4 jit_solution(11840816411865450984)
XLA Ops:
  13.7 32.6 %all-gather.6.cloned.1.call-done = bf16[128,5120]{1,0:T(8,128)(2,1)} async-done(((bf16[32,5120]{1,0:T(8,128)(2,1)}), bf16[128,5120]{1,0:T(8,128)(2,1)}) %all-gather.6.cloned.1.call-update) | async-done | bytes 1310736 | tf_op jit(solution)/shard_map/all_gather | solution.py:86
  46.3 3.4 fusion.60
  49.9 30.3 %all-gather.12.cloned.1.call-done = bf16[1,1,128,5120]{3,2,1,0:T(8,128)(2,1)} async-done(((bf16[1,1,32,5120]{3,2,1,0:T(8,128)(2,1)}), bf16[1,1,128,5120]{3,2,1,0:T(8,128)(2,1)}) %all-gather.12.cloned.1.call-update) | async-done | bytes 1310736 | tf_op jit(solution)/shard_map/all_gather | solution.py:87
  82.8 4.6 fusion.2
  90.1 27.9 %reduce-scatter.7.cloned.1.call-done = bf16[32,5120]{1,0:T(8,128)(2,1)} async-done(((bf16[128,5120]{1,0:T(8,128)(2,1)}), bf16[32,5120]{1,0:T(8,128)(2,1)}) %reduce-scatter.7.cloned.1.call-update) | async-done | bytes 327696 | tf_op jit(solution)/shard_map/reduce_scatter | solution.py:107
  123.4 2.8 fusion.75
  126.2 12.2 %collective-permute-done = bf16[32,5120]{1,0:T(8,128)(2,1)S(1)} collective-permute-done((bf16[32,5120]{1,0:T(8,128)(2,1)S(1)}, bf16[32,5120]{1,0:T(8,128)(2,1)S(1)}, u32[]{:S(2)}, u32[]{:S(2)}) %collective-permute-start) | collective-permute-done | bytes 327712 | tf_op jit(solution)/shard_map/ppermute | solution.py:18
  140.2 8.5 %collective-permute-done.1 = bf16[32,5120]{1,0:T(8,128)(2,1)S(1)} collective-permute-done((bf16[32,5120]{1,0:T(8,128)(2,1)S(1)}, bf16[32,5120]{1,0:T(8,128)(2,1)S(1)}, u32[]{:S(2)}, u32[]{:S(2)}) %collective-permute-start.1) | collective-permute-done | bytes 327712 | tf_op jit(solution)/shard_map/ppermute | solution.py:18
  151.3 2.6 convolution_convert_fusion.1
  154.7 28.8 %reduce-scatter.5.cloned.1.call-done = bf16[32,5120]{1,0:T(8,128)(2,1)} async-done(((bf16[128,5120]{1,0:T(8,128)(2,1)}), bf16[32,5120]{1,0:T(8,128)(2,1)}) %reduce-scatter.5.cloned.1.call-update) | async-done | bytes 327696 | tf_op jit(solution)/shard_map/reduce_scatter | solution.py:156
  185.8 3.4 collective-permute-start.3
  190.5 5.2 collective-permute-done.3
  195.7 8.9 %collective-permute-done.4 = bf16[32,5120]{1,0:T(8,128)(2,1)S(1)} collective-permute-done((bf16[32,5120]{1,0:T(8,128)(2,1)S(1)}, bf16[32,5120]{1,0:T(8,128)(2,1)S(1)}, u32[]{:S(2)}, u32[]{:S(2)}) %collective-permute-start.4) | collective-permute-done | bytes 327712 | tf_op jit(solution)/shard_map/ppermute | solution.py:27
  206.4 3.5 fusion.36
  209.9 5.0 fusion.33
  216.8 3.4 fusion.55
  220.4 30.1 %all-gather.8.cloned.1.call-done = bf16[128,5120]{1,0:T(8,128)(2,1)} async-done(((bf16[32,5120]{1,0:T(8,128)(2,1)}), bf16[128,5120]{1,0:T(8,128)(2,1)}) %all-gather.8.cloned.1.call-update) | async-done | bytes 1310736 | tf_op jit(solution)/shard_map/all_gather | solution.py:87
  253.8 3.5 fusion.30
  258.8 6.8 %fusion = bf16[3,5120,128]{1,2,0:T(8,128)(2,1)} fusion(f32[3,128,5120]{2,1,0:T(8,128)} %fusion.33, bf16[128,5120]{1,0:T(8,128)(2,1)} %all-gather.10.cloned.1.call-done, bf16[1,128,1,128]{3,1,2,0:T(8,128)(2,1)} %fusion.112, bf16[1,128,1,128]{3,1,2,0:T(8,128)(2,1)S(1)} %fusion.108, bf16[1,128,1,128]{3,1,2,0:T(8,128)(2,1)S(1)} %fusion.107), kind=kOutput, calls=%fused_computation.2 | convolution fusion | flops 507346944 | bytes 13205504 | tf_op jit(solution)/shard_map/sd,csn->cdn/dot_general | solution.py:120
  265.6 6.3 %copy.23 = bf16[3,5120,128]{2,1,0:T(8,128)(2,1)} copy(bf16[3,5120,128]{1,2,0:T(8,128)(2,1)} %fusion) | data formatting | bytes 7864320 | tf_op jit(solution)/shard_map/convert_element_type | solution.py:182
  271.9 13.0 %pad_maximum_fusion = bf16[2621440]{0:T(1024)(128)(2,1)S(1)} fusion(bf16[655360]{0:T(1024)(128)(2,1)S(1)} %bitcast.356, bf16[1966080]{0:T(1024)(128)(2,1)} %bitcast.354), kind=kLoop, calls=%fused_computation.17 | loop fusion | flops 10485760 | bytes 10485760 | tf_op jit(solution)/shard_map/concatenate | solution.py:181
  284.9 8.8 %collective-permute-done.8 = bf16[2621440]{0:T(1024)(128)(2,1)} collective-permute-done((bf16[2621440]{0:T(1024)(128)(2,1)S(1)}, bf16[2621440]{0:T(1024)(128)(2,1)}, u32[]{:S(2)}, u32[]{:S(2)}) %collective-permute-start.8) | collective-permute-done | bytes 5242912 | tf_op jit(solution)/shard_map/ppermute | solution.py:31
  295.2 2.4 fusion.3
  297.7 2.5 fusion.123
  300.1 27.2 %reduce-scatter.11.cloned.1.call-done = bf16[32,5120]{1,0:T(8,128)(2,1)} async-done(((bf16[128,5120]{1,0:T(8,128)(2,1)}), bf16[32,5120]{1,0:T(8,128)(2,1)}) %reduce-scatter.11.cloned.1.call-update) | async-done | bytes 327696 | tf_op jit(solution)/shard_map/reduce_scatter | solution.py:107
  328.7 2.2 fusion.137
  332.9 2.8 fusion.87
  335.7 12.2 %collective-permute-done.5 = bf16[32,5120]{1,0:T(8,128)(2,1)S(1)} collective-permute-done((bf16[32,5120]{1,0:T(8,128)(2,1)S(1)}, bf16[32,5120]{1,0:T(8,128)(2,1)S(1)}, u32[]{:S(2)}, u32[]{:S(2)}) %collective-permute-start.5) | collective-permute-done | bytes 327712 | tf_op jit(solution)/shard_map/ppermute | solution.py:18
  349.8 59.4 %collective-permute-done.9 = bf16[2621440]{0:T(1024)(128)(2,1)} collective-permute-done((bf16[2621440]{0:T(1024)(128)(2,1)}, bf16[2621440]{0:T(1024)(128)(2,1)}, u32[]{:S(2)}, u32[]{:S(2)}) %collective-permute-start.9) | collective-permute-done | bytes 5242912 | tf_op jit(solution)/shard_map/ppermute | solution.py:31
  415.6 27.8 %reduce-scatter.9.cloned.1.call-done = bf16[32,5120]{1,0:T(8,128)(2,1)} async-done(((bf16[128,5120]{1,0:T(8,128)(2,1)}), bf16[32,5120]{1,0:T(8,128)(2,1)}) %reduce-scatter.9.cloned.1.call-update) | async-done | bytes 327696 | tf_op jit(solution)/shard_map/reduce_scatter | solution.py:156
  445.5 78.2 %collective-permute-done.10 = bf16[2621440]{0:T(1024)(128)(2,1)} collective-permute-done((bf16[2621440]{0:T(1024)(128)(2,1)}, bf16[2621440]{0:T(1024)(128)(2,1)}, u32[]{:S(2)}, u32[]{:S(2)}) %collective-permute-start.10) | collective-permute-done | bytes 5242912 | tf_op jit(solution)/shard_map/ppermute | solution.py:31
  523.6 13.3 %add_convert_fusion = bf16[2621440]{0:T(1024)(128)(2,1)S(1)} fusion(bf16[2621440]{0:T(1024)(128)(2,1)} %collective-permute-done.10, bf16[655360]{0:T(1024)(128)(2,1)S(1)} %bitcast.357, bf16[1966080]{0:T(1024)(128)(2,1)} %bitcast.355), kind=kLoop, calls=%fused_computation | loop fusion | flops 18350080 | bytes 15728640 | tf_op jit(solution)/shard_map/convert_element_type | solution.py:188
  (145 shorter events, 53.5 us)
Async XLA Ops:
  7.2 73.0 %copy-start = (bf16[1,1,128,5120]{3,2,1,0:T(8,128)(2,1)S(1)}, bf16[1,1,128,5120]{3,2,1,0:T(8,128)(2,1)}, u32[]{:S(2)}) copy-start(bf16[1,1,128,5120]{3,2,1,0:T(8,128)(2,1)} %param.19) | copy-start | bytes 3932164
  7.2 39.1 %all-gather.6.cloned.1.call-start = ((), (), s32[]{:S(2)}) async-start(), calls=%async_computation.5 | async-start | bytes 1638400 | tf_op jit(solution)/shard_map/all_gather | solution.py:86
  10.9 69.3 %all-gather.12.cloned.1.call-start = ((), (), s32[]{:S(2)}) async-start(), calls=%async_computation.11 | async-start | bytes 1638400 | tf_op jit(solution)/shard_map/all_gather | solution.py:87
  12.9 105.2 %reduce-scatter.7.cloned.1.call-start = ((), (), s32[]{:S(2)}) async-start(), calls=%async_computation.6 | async-start | bytes 1638400 | tf_op jit(solution)/shard_map/reduce_scatter | solution.py:107
  82.8 35.2 %copy-start.4 = (bf16[1,1,2,32,5120]{4,3,2,1,0:T(8,128)(2,1)S(1)}, bf16[1,1,2,32,5120]{4,3,2,1,0:T(8,128)(2,1)}, u32[]{:S(2)}) copy-start(bf16[1,1,2,32,5120]{4,3,2,1,0:T(8,128)(2,1)} %param.22) | copy-start | bytes 1966084
  82.8 35.2 %copy-start.13 = (f32[1,1,5120]{2,1,0:T(1,128)S(1)}, f32[1,1,5120]{2,1,0:T(1,128)}, u32[]{:S(2)}) copy-start(f32[1,1,5120]{2,1,0:T(1,128)} %param.17) | copy-start | bytes 61444
  87.4 96.1 %reduce-scatter.5.cloned.1.call-start = ((), (), s32[]{:S(2)}) async-start(), calls=%async_computation.4 | async-start | bytes 1638400 | tf_op jit(solution)/shard_map/reduce_scatter | solution.py:156
  121.4 18.1 %collective-permute-start.2 = (bf16[32,5120]{1,0:T(8,128)(2,1)S(1)}, bf16[32,5120]{1,0:T(8,128)(2,1)S(1)}, u32[]{:S(2)}, u32[]{:S(2)}) collective-permute-start(bf16[32,5120]{1,0:T(8,128)(2,1)S(1)} %get-tuple-element.13), channel_id=1, source_target_pairs={{0,6},{2,0},{4,2},{6,4},{1,7},{3,1},{5,3},{7,5},{8,14},{10,8},{12,... | collective-permute-start | bytes 983048 | tf_op jit(solution)/shard_map/ppermute | solution.py:19
  122.5 15.9 %collective-permute-start = (bf16[32,5120]{1,0:T(8,128)(2,1)S(1)}, bf16[32,5120]{1,0:T(8,128)(2,1)S(1)}, u32[]{:S(2)}, u32[]{:S(2)}) collective-permute-start(bf16[32,5120]{1,0:T(8,128)(2,1)S(1)} %get-tuple-element.13), channel_id=1, source_target_pairs={{0,2},{2,4},{4,6},{6,0},{1,3},{3,5},{5,7},{7,1},{8,10},{10,12},{12... | collective-permute-start | bytes 983048 | tf_op jit(solution)/shard_map/ppermute | solution.py:18
  138.3 10.3 %collective-permute-start.1 = (bf16[32,5120]{1,0:T(8,128)(2,1)S(1)}, bf16[32,5120]{1,0:T(8,128)(2,1)S(1)}, u32[]{:S(2)}, u32[]{:S(2)}) collective-permute-start(bf16[32,5120]{1,0:T(8,128)(2,1)S(1)} %collective-permute-done), channel_id=1, source_target_pairs={{0,2},{2,4},{4,6},{6,0},{1,3},{3,5},{5,7},{7,1},{8,10},{10,12},{12... | collective-permute-start | bytes 983048 | tf_op jit(solution)/shard_map/ppermute | solution.py:18
  140.2 43.4 %copy-start.11 = (bf16[1,1,32,5120]{3,2,1,0:T(8,128)(2,1)S(1)}, bf16[1,1,32,5120]{3,2,1,0:T(8,128)(2,1)}, u32[]{:S(2)}) copy-start(bf16[1,1,32,5120]{3,2,1,0:T(8,128)(2,1)} %slice_select_fusion) | copy-start | bytes 983044
  140.2 43.4 %copy-start.12 = (bf16[32,5120]{1,0:T(8,128)(2,1)S(1)}, bf16[32,5120]{1,0:T(8,128)(2,1)}, u32[]{:S(2)}) copy-start(bf16[32,5120]{1,0:T(8,128)(2,1)} %reduce-scatter.7.cloned.1.call-done) | copy-start | bytes 983044
  153.9 62.9 %all-gather.10.cloned.1.call-start = ((), (), s32[]{:S(2)}) async-start(), calls=%async_computation.9 | async-start | bytes 1638400 | tf_op jit(solution)/shard_map/all_gather | solution.py:86
  154.7 95.8 %all-gather.8.cloned.1.call-start = ((), (), s32[]{:S(2)}) async-start(), calls=%async_computation.8 | async-start | bytes 1638400 | tf_op jit(solution)/shard_map/all_gather | solution.py:87
  183.6 21.8 %copy-start.14 = (bf16[1,2,32,5120]{3,2,1,0:T(8,128)(2,1)S(1)}, bf16[1,2,32,5120]{3,2,1,0:T(8,128)(2,1)}, u32[]{:S(2)}) copy-start(bf16[1,2,32,5120]{3,2,1,0:T(8,128)(2,1)} %param.23) | copy-start | bytes 1966084
  184.9 25.0 %copy-start.6 = (bf16[128,5120]{1,0:T(8,128)(2,1)S(1)}, bf16[128,5120]{1,0:T(8,128)(2,1)}, u32[]{:S(2)}) copy-start(bf16[128,5120]{1,0:T(8,128)(2,1)} %all-gather.6.cloned.1.call-done) | copy-start | bytes 3932164
  185.8 9.9 %collective-permute-start.3 = (bf16[32,5120]{1,0:T(8,128)(2,1)S(1)}, bf16[32,5120]{1,0:T(8,128)(2,1)S(1)}, u32[]{:S(2)}, u32[]{:S(2)}) collective-permute-start(bf16[32,5120]{1,0:T(8,128)(2,1)S(1)} %broadcast_select_fusion.1), channel_id=1, source_target_pairs={{0,8},{8,16},{16,24},{1,9},{9,17},{17,25},{2,10},{10,18},{18,26},{... | collective-permute-start | bytes 983048 | tf_op jit(solution)/shard_map/ppermute | solution.py:27
  189.2 15.5 %collective-permute-start.4 = (bf16[32,5120]{1,0:T(8,128)(2,1)S(1)}, bf16[32,5120]{1,0:T(8,128)(2,1)S(1)}, u32[]{:S(2)}, u32[]{:S(2)}) collective-permute-start(bf16[32,5120]{1,0:T(8,128)(2,1)S(1)} %get-tuple-element.7), channel_id=1, source_target_pairs={{8,0},{16,8},{24,16},{9,1},{17,9},{25,17},{10,2},{18,10},{26,18},{... | collective-permute-start | bytes 983048 | tf_op jit(solution)/shard_map/ppermute | solution.py:27
  206.2 121.1 %reduce-scatter.11.cloned.1.call-start = ((), (), s32[]{:S(2)}) async-start(), calls=%async_computation.10 | async-start | bytes 1638400 | tf_op jit(solution)/shard_map/reduce_scatter | solution.py:107
  271.9 23.3 %copy-start.2 = (bf16[1,1,3,5120,128]{4,3,2,1,0:T(8,128)(2,1)S(1)}, bf16[1,1,3,5120,128]{4,3,2,1,0:T(8,128)(2,1)}, u32[]{:S(2)}) copy-start(bf16[1,1,3,5120,128]{4,3,2,1,0:T(8,128)(2,1)} %param.18) | copy-start | bytes 11796484
  271.9 23.3 %copy-start.21 = (bf16[1,128,1,128]{3,1,2,0:T(8,128)(2,1)S(1)}, bf16[1,128,1,128]{3,1,2,0:T(8,128)(2,1)}, u32[]{:S(2)}) copy-start(bf16[1,128,1,128]{3,1,2,0:T(8,128)(2,1)} %fusion.112) | copy-start | bytes 98308
  284.8 43.8 %copy-start.23 = (f32[32]{0:T(128)S(1)}, f32[32]{0:T(128)}, u32[]{:S(2)}) copy-start(f32[32]{0:T(128)} %copy-done.22) | copy-start | bytes 388
  284.8 8.9 %collective-permute-start.8 = (bf16[2621440]{0:T(1024)(128)(2,1)S(1)}, bf16[2621440]{0:T(1024)(128)(2,1)}, u32[]{:S(2)}, u32[]{:S(2)}) collective-permute-start(bf16[2621440]{0:T(1024)(128)(2,1)S(1)} %pad_maximum_fusion), channel_id=1, source_target_pairs={{0,1},{1,0},{8,9},{9,8},{16,17},{17,16},{24,25},{25,24},{2,3},{3,2... | collective-permute-start | bytes 15728648 | tf_op jit(solution)/shard_map/ppermute | solution.py:31
  293.7 115.4 %collective-permute-start.9 = (bf16[2621440]{0:T(1024)(128)(2,1)}, bf16[2621440]{0:T(1024)(128)(2,1)}, u32[]{:S(2)}, u32[]{:S(2)}) collective-permute-start(bf16[2621440]{0:T(1024)(128)(2,1)} %collective-permute-done.8), channel_id=1, source_target_pairs={{0,8},{1,9},{8,0},{9,1},{16,24},{17,25},{24,16},{25,17},{2,10},{3,... | collective-permute-start | bytes 15728648 | tf_op jit(solution)/shard_map/ppermute | solution.py:31
  297.6 145.8 %reduce-scatter.9.cloned.1.call-start = ((), (), s32[]{:S(2)}) async-start(), calls=%async_computation.7 | async-start | bytes 1638400 | tf_op jit(solution)/shard_map/reduce_scatter | solution.py:156
  330.9 18.2 %collective-permute-start.7 = (bf16[32,5120]{1,0:T(8,128)(2,1)S(1)}, bf16[32,5120]{1,0:T(8,128)(2,1)S(1)}, u32[]{:S(2)}, u32[]{:S(2)}) collective-permute-start(bf16[32,5120]{1,0:T(8,128)(2,1)S(1)} %get-tuple-element.11), channel_id=1, source_target_pairs={{0,6},{2,0},{4,2},{6,4},{1,7},{3,1},{5,3},{7,5},{8,14},{10,8},{12,... | collective-permute-start | bytes 983048 | tf_op jit(solution)/shard_map/ppermute | solution.py:19
  332.0 15.9 %collective-permute-start.5 = (bf16[32,5120]{1,0:T(8,128)(2,1)S(1)}, bf16[32,5120]{1,0:T(8,128)(2,1)S(1)}, u32[]{:S(2)}, u32[]{:S(2)}) collective-permute-start(bf16[32,5120]{1,0:T(8,128)(2,1)S(1)} %get-tuple-element.11), channel_id=1, source_target_pairs={{0,2},{2,4},{4,6},{6,0},{1,3},{3,5},{5,7},{7,1},{8,10},{10,12},{12... | collective-permute-start | bytes 983048 | tf_op jit(solution)/shard_map/ppermute | solution.py:18
  347.9 62.7 %collective-permute-start.6 = (bf16[32,5120]{1,0:T(8,128)(2,1)S(1)}, bf16[32,5120]{1,0:T(8,128)(2,1)S(1)}, u32[]{:S(2)}, u32[]{:S(2)}) collective-permute-start(bf16[32,5120]{1,0:T(8,128)(2,1)S(1)} %collective-permute-done.5), channel_id=1, source_target_pairs={{0,2},{2,4},{4,6},{6,0},{1,3},{3,5},{5,7},{7,1},{8,10},{10,12},{12... | collective-permute-start | bytes 983048 | tf_op jit(solution)/shard_map/ppermute | solution.py:18
  349.1 62.6 %copy-start.26 = (s32[128]{0:T(128)S(1)}, s32[128]{0:T(128)}, u32[]{:S(2)}) copy-start(s32[128]{0:T(128)} %get-tuple-element.18) | copy-start | bytes 1540
  349.7 64.0 %copy-start.10 = (bf16[32,5120]{1,0:T(8,128)(2,1)S(1)}, bf16[32,5120]{1,0:T(8,128)(2,1)}, u32[]{:S(2)}) copy-start(bf16[32,5120]{1,0:T(8,128)(2,1)} %copy-done.9) | copy-start | bytes 983044
  409.1 114.5 %collective-permute-start.10 = (bf16[2621440]{0:T(1024)(128)(2,1)}, bf16[2621440]{0:T(1024)(128)(2,1)}, u32[]{:S(2)}, u32[]{:S(2)}) collective-permute-start(bf16[2621440]{0:T(1024)(128)(2,1)} %collective-permute-done.9), channel_id=1, source_target_pairs={{0,16},{1,17},{8,24},{9,25},{16,0},{17,1},{24,8},{25,9},{2,18},{3,... | collective-permute-start | bytes 15728648 | tf_op jit(solution)/shard_map/ppermute | solution.py:31
  411.2 33.4 %copy-start.8 = (bf16[32,5120]{1,0:T(8,128)(2,1)S(1)}, bf16[32,5120]{1,0:T(8,128)(2,1)}, u32[]{:S(2)}) copy-start(bf16[32,5120]{1,0:T(8,128)(2,1)} %copy-done.7) | copy-start | bytes 983044
  (15 other events, 84.9 us)
Sparse Core Ops, SparseCore 0:
  11.0 35.2 all-gather.5
  48.5 31.6 all-gather.11
  87.5 30.4 reduce-scatter.6
  154.0 29.4 reduce-scatter.4
  185.6 31.1 all-gather.9
  218.8 31.6 all-gather.7
  297.7 29.5 reduce-scatter.10
  413.8 29.5 reduce-scatter.8
